TPU v7x, 32 devices: a whole 2x2x4 slice. The times are simulated.
32 devices in a mesh: shard: 4 (over z), rep: 8 (over y, x, core).
Axes of the slice: x: 2, y: 2, z: 4, core: 2. Of those that a mesh axis runs over, the one named last changes fastest.
Arguments:
- grads: bfloat16 [1, 8192, 28672], P(None, 'shard', 'rep'), may hold values from -81 to 81
- seeds: int32 [1], replicated, may hold values from 0 to 999999
Outputs:
- projected: bfloat16 [512, 1, 28672], P('shard', None, 'rep')
All inputs are finite; a program needn't handle non-finite values.
Results may differ from a plain program's by a relative error of at most 0.0056.
Values may be sent and summed in bfloat16 or wider, within the bound.
No kernel may reach another device: no remote copies, remote signals or barrier semaphores. Data moves between devices by JAX's collectives and lax.ppermute only.
A program may use at most 128 MiB of HBM per device.

v0:
```python
import jax
import jax.numpy as jnp
from jax import lax
from jax.sharding import PartitionSpec as P

RANK = 512
mix_first = 668265263
mix_second = -2048144789
mix_third = -1028477387


def sketch_table(seeds, first_row, count, rank):
    rows = first_row + lax.iota(jnp.int32, count)
    columns = lax.iota(jnp.int32, rank)
    counter = rows[:, None] * jnp.int32(rank) + columns[None, :]
    hashed = jnp.bitwise_xor(counter[None, :, :], (seeds * jnp.int32(mix_first))[:, None, None])
    hashed = hashed * jnp.int32(mix_second)
    hashed = jnp.bitwise_xor(hashed, lax.shift_right_logical(hashed, jnp.int32(15)))
    hashed = hashed * jnp.int32(mix_third)
    hashed = jnp.bitwise_xor(hashed, lax.shift_right_logical(hashed, jnp.int32(13)))
    unit = lax.shift_right_logical(hashed, jnp.int32(8)).astype(jnp.float32) * (1.0 / 16777216.0)
    return (2.0 * unit - 1.0).astype(jnp.bfloat16)


def body(grads, seeds):
    mats, depth, width = grads.shape
    rows_whole = lax.all_to_all(grads, "rep", split_axis=1, concat_axis=2, tiled=True)
    block = rows_whole.shape[2] // 8

    def add_block(step, total):
        start = step * block
        table = sketch_table(seeds, start, block, RANK)
        piece = lax.dynamic_slice_in_dim(rows_whole, start, block, 2)
        return total + jnp.einsum("mdc,mcr->dmr", piece, table, preferred_element_type=jnp.float32)

    sketch_rows = lax.fori_loop(
        0, 8, add_block, jnp.zeros((rows_whole.shape[1], mats, RANK), jnp.float32)
    )
    local_gram = jnp.einsum(
        "dmr,dms->mrs",
        sketch_rows,
        sketch_rows,
        precision=lax.Precision.HIGHEST,
        preferred_element_type=jnp.float32,
    )
    gram = lax.psum(local_gram, ("shard", "rep"))
    factor = jnp.linalg.cholesky(gram)
    own_rows = jnp.transpose(sketch_rows, (1, 0, 2))
    basis_rows = lax.linalg.triangular_solve(
        factor, own_rows, left_side=False, lower=True, transpose_a=True
    ).astype(jnp.bfloat16)
    partial_sum = jnp.einsum(
        "mdr,mdc->rmc",
        lax.all_gather(basis_rows, "rep", axis=1, tiled=True),
        grads,
        preferred_element_type=jnp.float32,
    )
    projected = lax.psum_scatter(partial_sum, "shard", scatter_dimension=0, tiled=True)
    return projected.astype(jnp.bfloat16)


def solution(mesh):
    return jax.shard_map(
        body,
        mesh=mesh,
        in_specs=(P(None, "shard", "rep"), P()),
        out_specs=P("shard", None, "rep"),
        check_vma=False,
    )
```

profile of v0, /device:TPU:0, one launch (start us, length us, event | category | flops | bytes accessed | tf_op | source)
XLA Modules:
  0.0 861.6 jit_solution(14677463218900408071)
XLA Ops:
  6.5 26.0 %copy.30 = bf16[1,2048,3584]{2,0,1:T(2,128)(2,1)} copy(bf16[1,2048,3584]{2,1,0:T(8,128)(2,1)} %param.4) | data formatting | bytes 29360128 | tf_op args[0]
  33.1 94.1 %reduce.36 = bf16[2048,3584]{1,0:T(8,128)(2,1)} reduce(bf16[2048,1,3584]{2,1,0:T(2,128)(2,1)} %bitcast.210, bf16[]{:T(256)} %broadcast.502), dimensions={1}, to_apply=%bitcast.195.reduce_sub_computation | reduce | bytes 29360130
  127.2 16.3 %reshape.459 = bf16[8,2,458752]{2,1,0:T(2,128)(2,1)} reshape(bf16[2048,3584]{1,0:T(8,128)(2,1)} %reduce.36) | data formatting | bytes 29360128
  143.5 5.6 all-to-all-start
  149.9 161.3 %all-to-all-done = bf16[8,2,458752]{2,1,0:T(2,128)(2,1)} async-done(((bf16[8,2,458752]{2,1,0:T(2,128)(2,1)}), bf16[8,2,458752]{2,1,0:T(2,128)(2,1)}, u32[]{:S(2)}, u32[]{:S(2)}) %all-to-all-start) | async-done | bytes 14680096 | tf_op jit(solution)/shard_map/all_to_all | solution.py:27
  311.2 20.2 %reshape.460 = bf16[2048,1,3584]{2,1,0:T(2,128)(2,1)} reshape(bf16[8,2,458752]{2,1,0:T(2,128)(2,1)} %all-to-all-done) | data formatting | bytes 29360128
  331.4 19.4 %copy.28 = bf16[1,2048,3584]{2,1,0:T(8,128)(2,1)} copy(bf16[1,2048,3584]{2,0,1:T(2,128)(2,1)} %bitcast.211) | data formatting | bytes 29360128
  350.8 18.7 %copy.21 = bf16[1,256,8,3584]{1,3,2,0:T(8,128)(2,1)} copy(bf16[1,256,8,3584]{3,1,2,0:T(8,128)(2,1)} %bitcast.212) | data formatting | bytes 29360128 | tf_op jit(solution)/shard_map/all_to_all | solution.py:27
  369.5 42.8 %while.18 = (s32[]{:T(128)}, f32[256,1,512]{0,2,1:T(8,128)S(1)}, s32[1]{0:T(128)}, bf16[1,256,28672]{1,2,0:T(8,128)(2,1)}, s32[]{:T(128)}, /*index=5*/s32[]{:T(128)}, s32[]{:T(128)}, s32[]{:T(128)}) while((s32[]{:T(128)}, f32[256,1,512]{0,2,1:T(8,128)S(1)}, s32[1]{0:T(128)}, bf16[1,256,28672]{1,2,0:T(8,128)(2,1)}, s32[]{:T(128)}, ...), condition=%wide.region_1.0_spmd.clone, body=%wide.region_0.0_spmd.clone.sunk | while | flops 963648512 | bytes 2912917 | solution.py:36
  369.5 5.3 fusion.77
  374.8 5.3 fusion.77
  380.2 5.3 fusion.77
  385.5 5.3 fusion.77
  390.9 5.3 fusion.77
  396.2 5.3 fusion.77
  401.6 5.3 fusion.77
  407.0 5.3 fusion.77
  412.3 2.1 convolution_bitcast_fusion
  414.9 130.6 %all-reduce.3.cloned.1.call-done = f32[1,512,512]{1,2,0:T(8,128)} async-done(((f32[1,512,512]{1,2,0:T(8,128)}), f32[1,512,512]{1,2,0:T(8,128)}) %all-reduce.3.cloned.1.call-update) | async-done | bytes 1048592 | tf_op jit(solution)/shard_map/psum | solution.py:46
  545.5 1.6 copy.25
  547.1 1.4 fusion.47
  548.5 11.7 %custom-call.34 = f32[1,128,128]{2,1,0:T(8,128)S(1)} custom-call(f32[1,128,128]{2,1,0:T(8,128)S(1)} %cholesky.267), custom_call_target="Cholesky" | custom-call | tf_op jit(solution)/shard_map/jit(cholesky)/cholesky | solution.py:47
  560.3 9.8 %custom-call.35 = f32[1,1,128,128]{2,3,1,0:T(8,128)S(1)} custom-call(f32[1,1,128,128]{3,2,1,0:T(8,128)S(1)} %get-tuple-element.173), custom_call_target="InvertDiagBlocksLowerTriangular" | custom-call | tf_op jit(solution)/shard_map/jit(cholesky)/cholesky | solution.py:47
  570.9 11.7 %custom-call.36 = f32[1,128,128]{2,1,0:T(8,128)S(1)} custom-call(f32[1,128,128]{2,1,0:T(8,128)S(1)} %cholesky.271), custom_call_target="Cholesky" | custom-call | tf_op jit(solution)/shard_map/jit(cholesky)/cholesky | solution.py:47
  582.6 10.2 %custom-call.37 = f32[1,1,128,128]{2,3,1,0:T(8,128)S(1)} custom-call(f32[1,1,128,128]{3,2,1,0:T(8,128)S(1)} %get-tuple-element.170), custom_call_target="InvertDiagBlocksLowerTriangular" | custom-call | tf_op jit(solution)/shard_map/jit(cholesky)/cholesky | solution.py:47
  593.5 11.7 %custom-call.38 = f32[1,128,128]{2,1,0:T(8,128)S(1)} custom-call(f32[1,128,128]{2,1,0:T(8,128)S(1)} %cholesky.276), custom_call_target="Cholesky" | custom-call | tf_op jit(solution)/shard_map/jit(cholesky)/cholesky | solution.py:47
  605.2 0.7 compare_reduce_fusion.1
  606.0 9.8 %custom-call.39 = f32[1,1,128,128]{2,3,1,0:T(8,128)S(1)} custom-call(f32[1,1,128,128]{3,2,1,0:T(8,128)S(1)} %get-tuple-element.167), custom_call_target="InvertDiagBlocksLowerTriangular" | custom-call | tf_op jit(solution)/shard_map/jit(cholesky)/cholesky | solution.py:47
  616.4 11.7 %custom-call.40 = f32[1,128,128]{2,1,0:T(8,128)S(1)} custom-call(f32[1,128,128]{2,1,0:T(8,128)S(1)} %fusion.46), custom_call_target="Cholesky" | custom-call | tf_op jit(solution)/shard_map/jit(cholesky)/cholesky | solution.py:47
  628.1 0.6 compare_reduce_fusion
  628.8 0.9 compare_reduce_fusion.2
  632.3 8.1 while.17
  632.4 0.6 fusion.74
  633.0 1.3 bitcast_dynamic-update-slice_fusion.2
  634.4 0.6 fusion.74
  635.0 1.3 bitcast_dynamic-update-slice_fusion.2
  636.5 0.6 fusion.74
  637.1 1.3 bitcast_dynamic-update-slice_fusion.2
  638.5 0.6 fusion.74
  639.1 1.3 bitcast_dynamic-update-slice_fusion.2
  640.4 39.3 %custom-call.41 = f32[1,4,128,128]{2,3,1,0:T(8,128)S(1)} custom-call(f32[1,4,128,128]{3,2,1,0:T(8,128)S(1)} %bitcast.221), custom_call_target="InvertDiagBlocksLowerTriangular" | custom-call | tf_op jit(solution)/shard_map/triangular_solve | solution.py:49
  680.8 0.6 fusion.41
  681.7 0.8 fusion.43
  682.9 0.7 pad_maximum_fusion
  683.7 27.2 %all-gather.2.cloned.1.call-done = bf16[1,2048,512]{1,2,0:T(8,128)(2,1)} async-done(((bf16[1,256,512]{1,2,0:T(8,128)(2,1)}), bf16[1,2048,512]{1,2,0:T(8,128)(2,1)}) %all-gather.2.cloned.1.call-update) | async-done | bytes 2097168 | tf_op jit(solution)/shard_map/all_gather | solution.py:54
  710.9 13.5 %fusion.31 = f32[512,1,3584]{2,0,1:T(8,128)} fusion(bf16[1,2048,3584]{2,1,0:T(8,128)(2,1)} %param.4, bf16[1,2048,512]{1,2,0:T(8,128)(2,1)} %all-gather.2.cloned.1.call-done), kind=kOutput, calls=%fused_computation.27 | convolution fusion | flops 7516192768 | bytes 24117248 | tf_op jit(solution)/shard_map/mdr,mdc->rmc/dot_general | solution.py:52
  724.4 127.9 %reduce-scatter.2.cloned.1.call-done = f32[128,1,3584]{2,0,1:T(8,128)} async-done(((f32[512,1,3584]{2,0,1:T(8,128)}), f32[128,1,3584]{2,0,1:T(8,128)}) %reduce-scatter.2.cloned.1.call-update) | async-done | bytes 1835024 | tf_op jit(solution)/shard_map/reduce_scatter | solution.py:58
  852.3 2.5 convert_element_type.66
  (44 shorter events, 5.6 us)
Async XLA Ops:
  143.5 167.7 %all-to-all-start = ((bf16[8,2,458752]{2,1,0:T(2,128)(2,1)}), bf16[8,2,458752]{2,1,0:T(2,128)(2,1)}, u32[]{:S(2)}, u32[]{:S(2)}) async-start(bf16[8,2,458752]{2,1,0:T(2,128)(2,1)} %reshape.459), calls=%async_computation | async-start | bytes 29360128 | tf_op jit(solution)/shard_map/all_to_all | solution.py:27
  149.1 396.4 %all-reduce.3.cloned.1.call-start = ((), (), s32[]{:S(2)}) async-start(), calls=%async_computation.2 | async-start | bytes 2097152 | tf_op jit(solution)/shard_map/psum | solution.py:46
  414.4 296.5 %all-gather.2.cloned.1.call-start = ((), (), s32[]{:S(2)}) async-start(), calls=%async_computation.3 | async-start | bytes 2359296 | tf_op jit(solution)/shard_map/all_gather | solution.py:54
  683.6 168.7 %reduce-scatter.2.cloned.1.call-start = ((), (), s32[]{:S(2)}) async-start(), calls=%async_computation.4 | async-start | bytes 9175040 | tf_op jit(solution)/shard_map/reduce_scatter | solution.py:58
Sparse Core Ops, SparseCore 0:
  414.5 130.9 all-reduce.2
  683.8 27.0 all-gather.1
  724.5 127.7 reduce-scatter.1
where the time goes:
time: 869 us; the launch traced here: 862 us
  waiting for transfers between devices  447 us (51%)
  other arithmetic  217 us (25%)
  local copies, waits for them, and re-layouts  111 us (13%)
  matrix products  63 us (7%)
  between operations  16.7 us (2%)
    all_to_all x1, waiting for transfers between devices, body(): lax.all_to_all(grads, 'rep', split_axis=1, concat_axis=2, tiled=True)  161 us
    psum x1, waiting for transfers between devices, body(): gram = lax.psum(local_gram, ('shard', 'rep'))  131 us
    reduce_scatter x1, waiting for transfers between devices, body(): lax.psum_scatter(partial_sum, 'shard', scatter_dimension=0, tiled=True)  128 us
    unnamed x3, other arithmetic  94.1 us
    unnamed x5, local copies, waits for them, and re-layouts  82.4 us
    another operation x14, other arithmetic, body(): factor = jnp.linalg.cholesky(gram)  79 us
    dot_general x8, matrix products, add_block(): jnp.einsum('mdc,mcr->dmr', piece, table, preferred_element_type=jnp.float32)  42.5 us
    another operation x4, other arithmetic, body(): lax.linalg.triangular_solve(factor, own_rows, left_side=False, lower=True...  40.2 us
  transfers between devices with their start and end apart: 4, of which 4 were waited for; matrix products, arithmetic and copies ran while one was open for 0% of the time, Pallas kernels for 0%

commit v1 on v0

--- a/solution.py
+++ b/solution.py
@@ -49,12 +49,22 @@
     basis_rows = lax.linalg.triangular_solve(
         factor, own_rows, left_side=False, lower=True, transpose_a=True
     ).astype(jnp.bfloat16)
-    partial_sum = jnp.einsum(
-        "mdr,mdc->rmc",
-        lax.all_gather(basis_rows, "rep", axis=1, tiled=True),
-        grads,
-        preferred_element_type=jnp.float32,
-    )
+    devices, index, rows_2 = (lax.axis_size("rep"), lax.axis_index("rep"), basis_rows.shape[1])
+    right = [(i, (i + 1) % devices) for i in range(devices)]
+    carried, total_2 = (basis_rows, None)
+    for turn in range(devices):
+        coming = lax.ppermute(carried, "rep", right) if turn < devices - 1 else None
+        update = jnp.einsum(
+            "mdr,mdc->rmc",
+            carried,
+            lax.dynamic_slice_in_dim(
+                grads, (index - turn) % devices * rows_2, carried.shape[1], axis=1
+            ),
+            preferred_element_type=jnp.float32,
+        )
+        total_2 = update if total_2 is None else total_2 + update
+        carried = coming
+    partial_sum = total_2
     projected = lax.psum_scatter(partial_sum, "shard", scatter_dimension=0, tiled=True)
     return projected.astype(jnp.bfloat16)
 

time: 869 us -> 902 us (1.038)
  matrix products: 63 us -> 106 us
  waiting for transfers between devices: 447 us -> 431 us
    dot_general x1 -> x8, matrix products: 13.5 us -> 53.3 us  [body(): jnp.einsum('mdr,mdc->rmc', carried, lax.dynamic_slice_in_dim(grads, (inde...]
    all_gather x1 -> x0, waiting for transfers between devices: 27.2 us -> none  [body(): lax.all_gather(basis_rows, 'rep', axis=1, tiled=True)]
    ppermute x0 -> x7, waiting for transfers between devices: none -> 13.8 us  [body(): coming = lax.ppermute(carried, 'rep', right) if turn < devices - 1 else None]
    unnamed x5 -> x13, local copies, waits for them, and re-layouts: 82.4 us -> 82.5 us
    unnamed x3 -> x4, other arithmetic: 94.1 us -> 94.1 us
  transfers between devices with their start and end apart: 4 -> 10, of which waited for: 4 -> 10; matrix products, arithmetic and copies ran while one was open for 0% -> 4% of each run, Pallas kernels for 0% -> 0%
where the time goes in v1:
time: 902 us; the launch traced here: 894 us
  waiting for transfers between devices  431 us (48%)
  other arithmetic  216 us (24%)
  local copies, waits for them, and re-layouts  116 us (13%)
  matrix products  106 us (12%)
  between operations  17.2 us (2%)
    all_to_all x1, waiting for transfers between devices, body(): lax.all_to_all(grads, 'rep', split_axis=1, concat_axis=2, tiled=True)  161 us
    psum x1, waiting for transfers between devices, body(): gram = lax.psum(local_gram, ('shard', 'rep'))  130 us
    reduce_scatter x1, waiting for transfers between devices, body(): lax.psum_scatter(partial_sum, 'shard', scatter_dimension=0, tiled=True)  127 us
    unnamed x4, other arithmetic  94.1 us
    unnamed x13, local copies, waits for them, and re-layouts  82.5 us
    another operation x14, other arithmetic, body(): factor = jnp.linalg.cholesky(gram)  78.9 us
    dot_general x8, matrix products, body(): jnp.einsum('mdr,mdc->rmc', carried, lax.dynamic_slice_in_dim(grads, (inde...  53.3 us
    dot_general x8, matrix products, add_block(): jnp.einsum('mdc,mcr->dmr', piece, table, preferred_element_type=jnp.float32)  42.5 us
  transfers between devices with their start and end apart: 10, of which 10 were waited for; matrix products, arithmetic and copies ran while one was open for 4% of the time, Pallas kernels for 0%

profile of v1, /device:TPU:0, one launch (start us, length us, event | category | flops | bytes accessed | tf_op | source)
XLA Modules:
  0.0 894.3 jit_solution(12096489681459545140)
XLA Ops:
  6.5 26.0 %copy.35 = bf16[1,2048,3584]{2,0,1:T(2,128)(2,1)} copy(bf16[1,2048,3584]{2,1,0:T(8,128)(2,1)} %param.4) | data formatting | bytes 29360128 | tf_op args[0]
  33.1 94.1 %reduce.36 = bf16[2048,3584]{1,0:T(8,128)(2,1)} reduce(bf16[2048,1,3584]{2,1,0:T(2,128)(2,1)} %bitcast.244, bf16[]{:T(256)} %broadcast.510), dimensions={1}, to_apply=%bitcast.229.reduce_sub_computation | reduce | bytes 29360130
  127.2 16.2 %reshape.534 = bf16[8,2,458752]{2,1,0:T(2,128)(2,1)} reshape(bf16[2048,3584]{1,0:T(8,128)(2,1)} %reduce.36) | data formatting | bytes 29360128
  143.5 5.6 all-to-all-start
  149.9 161.3 %all-to-all-done = bf16[8,2,458752]{2,1,0:T(2,128)(2,1)} async-done(((bf16[8,2,458752]{2,1,0:T(2,128)(2,1)}), bf16[8,2,458752]{2,1,0:T(2,128)(2,1)}, u32[]{:S(2)}, u32[]{:S(2)}) %all-to-all-start) | async-done | bytes 14680096 | tf_op jit(solution)/shard_map/all_to_all | solution.py:27
  311.2 20.2 %reshape.535 = bf16[2048,1,3584]{2,1,0:T(2,128)(2,1)} reshape(bf16[8,2,458752]{2,1,0:T(2,128)(2,1)} %all-to-all-done) | data formatting | bytes 29360128
  331.4 19.4 %copy.33 = bf16[1,2048,3584]{2,1,0:T(8,128)(2,1)} copy(bf16[1,2048,3584]{2,0,1:T(2,128)(2,1)} %bitcast.245) | data formatting | bytes 29360128
  350.8 18.7 %copy.25 = bf16[1,256,8,3584]{1,3,2,0:T(8,128)(2,1)} copy(bf16[1,256,8,3584]{3,1,2,0:T(8,128)(2,1)} %bitcast.246) | data formatting | bytes 29360128 | tf_op jit(solution)/shard_map/all_to_all | solution.py:27
  369.5 42.8 %while.18 = (s32[]{:T(128)}, f32[256,1,512]{0,2,1:T(8,128)S(1)}, s32[1]{0:T(128)}, bf16[1,256,28672]{1,2,0:T(8,128)(2,1)}, s32[]{:T(128)}, /*index=5*/s32[]{:T(128)}, s32[]{:T(128)}, s32[]{:T(128)}) while((s32[]{:T(128)}, f32[256,1,512]{0,2,1:T(8,128)S(1)}, s32[1]{0:T(128)}, bf16[1,256,28672]{1,2,0:T(8,128)(2,1)}, s32[]{:T(128)}, ...), condition=%wide.region_1.0_spmd.clone, body=%wide.region_0.0_spmd.clone.sunk | while | flops 963648512 | bytes 2912925 | solution.py:36
  369.5 5.3 fusion.119
  374.8 5.3 fusion.119
  380.2 5.3 fusion.119
  385.6 5.3 fusion.119
  390.9 5.3 fusion.119
  396.3 5.3 fusion.119
  401.6 5.3 fusion.119
  407.0 5.3 fusion.119
  412.3 2.1 convolution_bitcast_fusion
  415.9 129.5 %all-reduce.3.cloned.1.call-done = f32[1,512,512]{1,2,0:T(8,128)} async-done(((f32[1,512,512]{1,2,0:T(8,128)}), f32[1,512,512]{1,2,0:T(8,128)}) %all-reduce.3.cloned.1.call-update) | async-done | bytes 1048592 | tf_op jit(solution)/shard_map/psum | solution.py:46
  548.4 11.7 %custom-call.34 = f32[1,128,128]{2,1,0:T(8,128)S(1)} custom-call(f32[1,128,128]{2,1,0:T(8,128)S(1)} %cholesky.267), custom_call_target="Cholesky" | custom-call | tf_op jit(solution)/shard_map/jit(cholesky)/cholesky | solution.py:47
  560.2 9.8 %custom-call.35 = f32[1,1,128,128]{2,3,1,0:T(8,128)S(1)} custom-call(f32[1,1,128,128]{3,2,1,0:T(8,128)S(1)} %get-tuple-element.179), custom_call_target="InvertDiagBlocksLowerTriangular" | custom-call | tf_op jit(solution)/shard_map/jit(cholesky)/cholesky | solution.py:47
  570.8 11.7 %custom-call.36 = f32[1,128,128]{2,1,0:T(8,128)S(1)} custom-call(f32[1,128,128]{2,1,0:T(8,128)S(1)} %cholesky.271), custom_call_target="Cholesky" | custom-call | tf_op jit(solution)/shard_map/jit(cholesky)/cholesky | solution.py:47
  582.5 10.2 %custom-call.37 = f32[1,1,128,128]{2,3,1,0:T(8,128)S(1)} custom-call(f32[1,1,128,128]{3,2,1,0:T(8,128)S(1)} %get-tuple-element.176), custom_call_target="InvertDiagBlocksLowerTriangular" | custom-call | tf_op jit(solution)/shard_map/jit(cholesky)/cholesky | solution.py:47
  593.4 11.7 %custom-call.38 = f32[1,128,128]{2,1,0:T(8,128)S(1)} custom-call(f32[1,128,128]{2,1,0:T(8,128)S(1)} %cholesky.276), custom_call_target="Cholesky" | custom-call | tf_op jit(solution)/shard_map/jit(cholesky)/cholesky | solution.py:47
  605.9 9.8 %custom-call.39 = f32[1,1,128,128]{2,3,1,0:T(8,128)S(1)} custom-call(f32[1,1,128,128]{3,2,1,0:T(8,128)S(1)} %get-tuple-element.173), custom_call_target="InvertDiagBlocksLowerTriangular" | custom-call | tf_op jit(solution)/shard_map/jit(cholesky)/cholesky | solution.py:47
  616.3 11.8 %custom-call.40 = f32[1,128,128]{2,1,0:T(8,128)S(1)} custom-call(f32[1,128,128]{2,1,0:T(8,128)S(1)} %fusion.62), custom_call_target="Cholesky" | custom-call | tf_op jit(solution)/shard_map/jit(cholesky)/cholesky | solution.py:47
  632.0 10.5 %while.17 = (s32[]{:T(128)}, f32[1,512,512]{2,1,0:T(8,128)S(1)}, s32[4,2]{0,1:T(2,128)S(1)}, f32[4,1,128,128]{3,2,1,0:T(8,128)}, s32[]{:T(128)}) while((s32[]{:T(128)}, f32[1,512,512]{2,1,0:T(8,128)S(1)}, s32[4,2]{0,1:T(2,128)S(1)}, f32[4,1,128,128]{3,2,1,0:T(8,128)}, s32[]{:T(128)}) %tuple.72), condition=%wide.while_cond, body=%wide.while_body.sunk | while | flops 2 | bytes 132205 | solution.py:49
  632.7 2.0 bitcast_dynamic-update-slice_fusion.2
  635.3 2.0 bitcast_dynamic-update-slice_fusion.2
  637.9 2.0 bitcast_dynamic-update-slice_fusion.2
  640.5 2.0 bitcast_dynamic-update-slice_fusion.2
  642.5 40.1 %custom-call.41 = f32[1,4,128,128]{2,3,1,0:T(8,128)S(1)} custom-call(f32[1,4,128,128]{3,2,1,0:T(8,128)} %bitcast.261), custom_call_target="InvertDiagBlocksLowerTriangular" | custom-call | tf_op jit(solution)/shard_map/triangular_solve | solution.py:49
  687.3 1.7 fusion.60
  689.5 5.8 fusion.42
  696.8 5.7 fusion.40
  702.9 4.2 fusion.38
  707.0 2.5 collective-permute-done.2
  709.5 4.1 fusion.36
  713.6 2.6 collective-permute-done.3
  716.2 4.2 fusion.34
  720.4 2.5 collective-permute-done.4
  723.1 4.1 fusion.32
  727.3 2.5 collective-permute-done.5
  729.8 4.2 fusion.30
  734.0 2.5 collective-permute-done.6
  736.5 21.0 %add_bitcast_fusion = f32[512,1,3584]{0,2,1:T(8,128)} fusion(f32[3584,512]{1,0:T(8,128)} %fusion.30, f32[3584,512]{1,0:T(8,128)} %fusion.32, f32[3584,512]{1,0:T(8,128)} %fusion.34, f32[3584,512]{1,0:T(8,128)} %fusion.36, f32[3584,512]{1,0:T(8,128)} %fusion.38, f32[3584,512]{1,0:T(8,128)} %fusion.42, f32[3584,512]{1,0:T(8,128)} %fusion.40, ...), kind=kOutput, calls=%fused_computation.25 | convolution fusion | flops 952369152 | bytes 60817412 | tf_op jit(solution)/shard_map/mdr,mdc->rmc/dot_general | solution.py:57
  757.6 126.8 %reduce-scatter.2.cloned.1.call-done = f32[128,1,3584]{0,2,1:T(8,128)} async-done(((f32[512,1,3584]{0,2,1:T(8,128)}), f32[128,1,3584]{0,2,1:T(8,128)}) %reduce-scatter.2.cloned.1.call-update) | async-done | bytes 1835024 | tf_op jit(solution)/shard_map/reduce_scatter | solution.py:68
  884.4 1.6 convert_element_type.67
  (72 shorter events, 20.4 us)
Async XLA Ops:
  143.5 167.7 %all-to-all-start = ((bf16[8,2,458752]{2,1,0:T(2,128)(2,1)}), bf16[8,2,458752]{2,1,0:T(2,128)(2,1)}, u32[]{:S(2)}, u32[]{:S(2)}) async-start(bf16[8,2,458752]{2,1,0:T(2,128)(2,1)} %reshape.534), calls=%async_computation | async-start | bytes 29360128 | tf_op jit(solution)/shard_map/all_to_all | solution.py:27
  149.0 396.3 %all-reduce.3.cloned.1.call-start = ((), (), s32[]{:S(2)}) async-start(), calls=%async_computation.2 | async-start | bytes 2097152 | tf_op jit(solution)/shard_map/psum | solution.py:46
  414.4 470.0 %reduce-scatter.2.cloned.1.call-start = ((), (), s32[]{:S(2)}) async-start(), calls=%async_computation.3 | async-start | bytes 9175040 | tf_op jit(solution)/shard_map/reduce_scatter | solution.py:68
  632.0 70.9 %slice-start = ((s8[14680064]{0:T(1024)(128)(4,1)}), s8[2097152]{0:T(1024)(128)(4,1)S(1)}, s32[]{:S(2)}) async-start(s8[14680064]{0:T(1024)(128)(4,1)} %bitcast.247), calls=%async_computation.4 | async-start | bytes 4194304
  689.4 6.7 collective-permute-start
  689.5 13.4 %slice-start.1 = ((s8[14680064]{0:T(1024)(128)(4,1)}), s8[4194304]{0:T(1024)(128)(4,1)S(1)}, s32[]{:S(2)}) async-start(s8[14680064]{0:T(1024)(128)(4,1)} %bitcast.247), calls=%async_computation.5 | async-start | bytes 8388608
  689.5 13.4 %slice-start.2 = ((s8[14680064]{0:T(1024)(128)(4,1)}), s8[4194304]{0:T(1024)(128)(4,1)S(1)}, s32[]{:S(2)}) async-start(s8[14680064]{0:T(1024)(128)(4,1)} %bitcast.247), calls=%async_computation.6 | async-start | bytes 8388608
  695.3 7.6 slice-start.3
  696.1 6.7 collective-permute-start.1
  702.8 6.7 collective-permute-start.2
  709.5 6.7 collective-permute-start.3
  716.2 6.7 collective-permute-start.4
  722.9 6.9 collective-permute-start.5
  729.8 6.7 collective-permute-start.6
Sparse Core Ops, SparseCore 0:
  414.5 130.8 all-reduce.2
  757.7 126.6 reduce-scatter.1
